TPU v7x, 32 devices: a whole 2x2x4 slice. The times are simulated.
32 devices in a mesh: pw: 8 (over z, y), band: 4 (over x, core).
Axes of the slice: x: 2, y: 2, z: 4, core: 2. Of those that a mesh axis runs over, the one named last changes fastest.
Arguments:
- psi_block: float32 [2, 8, 256, 128], P(None, 'band', 'pw'), may hold values from -6 to 6
- psi_all: bfloat16 [2, 1024, 256, 128], P(None, 'band', 'pw'), may hold values from -0.0234375 to 0.0234375
- potential: float32 [128, 128, 128], P('pw'), may hold values from -8 to 8
- stick_col: int32 [256], replicated, may hold values from 0 to 16383, as said below
Outputs:
- intersection: float32 [2, 8, 1024], P(None, 'pw', 'band')
- hpsi: float32 [2, 8, 256, 128], P(None, 'band', 'pw')
Inputs may be any that keep to these rules, and one draw needn't show every extreme that they name: `stick_col`: distinct columns of the 128 x 128 plane; column 0 and column 16383 are always among them.
All inputs are finite; a program needn't handle non-finite values.
Results may differ from a plain program's by a relative error of at most 0.0029.
Values may be sent and summed in bfloat16 or wider, within the bound.
No kernel may reach another device: no remote copies, remote signals or barrier semaphores. Data moves between devices by JAX's collectives and lax.ppermute only.
A program may use at most 64 MiB of HBM per device.

v0:
```python
import math
import jax
import numpy as np
import jax.numpy as jnp
from jax import lax
from jax.sharding import PartitionSpec as P


def frequency(index, size):
    return jnp.where(index < size // 2, index, index - size)


def kinetic_table(columns, grid_size):
    col_x = frequency(columns // grid_size, grid_size).astype(jnp.float32)
    col_y = frequency(columns % grid_size, grid_size).astype(jnp.float32)
    along = frequency(jnp.arange(grid_size, dtype=jnp.int32), grid_size).astype(jnp.float32)
    plane = col_x * col_x + col_y * col_y
    return 4.0 * (plane[:, None] + along[None, :] * along[None, :]) / float(grid_size * grid_size)


def dft_table(grid_size, sign):
    indices = np.arange(grid_size)
    products = indices[:, None] * indices[None, :] % grid_size
    angles = 2.0 * np.pi / grid_size * products
    cosine = np.cos(angles)
    sine = sign * np.sin(angles)
    table = np.stack([np.stack([cosine, -sine]), np.stack([sine, cosine])])
    return jnp.asarray(table.astype(np.float32))


def plane_tables(stick_col, grid_size):
    grid_iota = jnp.arange(grid_size, dtype=jnp.int32)
    col_x = stick_col // grid_size
    col_y = stick_col % grid_size
    phase_angles = (
        2.0
        * math.pi
        / grid_size
        * (grid_iota[:, None] * col_x[None, :] % grid_size).astype(jnp.float32)
    )
    place_cols = (col_y[:, None] == grid_iota[None, :]).astype(jnp.float32)
    pick_cols = (grid_iota[:, None] == col_y[None, :]).astype(jnp.float32)
    return (jnp.cos(phase_angles), jnp.sin(phase_angles), place_cols, pick_cols)


def mult(left, right):
    return jnp.dot(left, right, precision=lax.Precision.HIGH, preferred_element_type=jnp.float32)


def plane_phase(amp, pot, tables, grid_size):
    phase_cos, phase_sin, place_cols, pick_cols = tables
    inverse = dft_table(grid_size, 1.0)
    cosine = inverse[0, 0]
    sine = inverse[1, 0]
    scaled_pot = (pot / float(grid_size**3))[None]
    val_re = amp[0][:, :, None, :]
    val_im = amp[1][:, :, None, :]
    spread_re = val_re * phase_cos - val_im * phase_sin
    spread_im = val_re * phase_sin + val_im * phase_cos
    rows_re = mult(spread_re, place_cols)
    rows_im = mult(spread_im, place_cols)
    shared = mult(rows_re + rows_im, cosine)
    wave_re = (shared - mult(rows_im, cosine + sine)) * scaled_pot
    wave_im = (shared + mult(rows_re, sine - cosine)) * scaled_pot
    shared = mult(wave_re + wave_im, cosine)
    back_re = shared - mult(wave_im, cosine - sine)
    back_im = shared - mult(wave_re, sine + cosine)
    sel_re = mult(back_re, pick_cols)
    sel_im = mult(back_im, pick_cols)
    picked_re = jnp.sum(sel_re * phase_cos + sel_im * phase_sin, axis=2)
    picked_im = jnp.sum(sel_im * phase_cos - sel_re * phase_sin, axis=2)
    return jnp.stack([picked_re, picked_im])


def intersect(lowered, psi_all, pw_count):
    turned = jnp.stack([-lowered[1], lowered[0]])
    both = jnp.concatenate([lowered, turned], axis=1)
    dims = (((2, 3), (2, 3)), ((0,), (0,)))
    width = psi_all.shape[1] // 4
    partial_value = jnp.concatenate(
        [
            jnp.sum(
                lax.dot_general(
                    both,
                    psi_all[:, k * width : (k + 1) * width],
                    dims,
                    preferred_element_type=jnp.float32,
                ),
                axis=0,
            )
            for k in range(4)
        ],
        axis=-1,
    )
    partial_value = partial_value.reshape(2, lowered.shape[1], partial_value.shape[-1])
    rows_dev = partial_value.shape[1] // pw_count
    pieces = partial_value.reshape(2, pw_count, rows_dev, partial_value.shape[-1])
    pieces = lax.all_to_all(pieces, "pw", split_axis=1, concat_axis=1, tiled=True)
    return jnp.sum(pieces, axis=1)


def per_device_rows(psi_block, psi_all, potential, stick_col):
    sticks_dev = psi_block.shape[2]
    grid_size = psi_block.shape[3]
    fast = lax.Precision.HIGH
    rank = lax.axis_index("pw")
    pw_count = lax.axis_size("pw")
    planes = potential.shape[0]
    my_columns = lax.dynamic_slice_in_dim(stick_col, rank * sticks_dev, sticks_dev)
    kinetic = kinetic_table(my_columns, grid_size)
    inverse = dft_table(grid_size, 1.0)
    forward = dft_table(grid_size, -1.0)
    tables = plane_tables(stick_col, grid_size)
    parts = []
    for band in range(psi_block.shape[1]):
        coeffs = psi_block[:, band : band + 1]
        z_lines = jnp.einsum("dczk,cbsk->zdbs", inverse, coeffs, precision=fast)
        received = lax.all_to_all(z_lines, "pw", split_axis=0, concat_axis=0, tiled=True)
        lanes = received.shape[1:]
        received = received.reshape((pw_count, planes) + lanes)
        amp = jnp.transpose(received, (2, 3, 1, 0, 4)).reshape(
            lanes[0], lanes[1], planes, pw_count * sticks_dev
        )
        picked = plane_phase(amp, potential, tables, grid_size)
        outgoing = picked.reshape(lanes[0], lanes[1], planes, pw_count, sticks_dev)
        outgoing = jnp.transpose(outgoing, (3, 2, 0, 1, 4)).reshape((pw_count * planes,) + lanes)
        sticks_back = lax.all_to_all(outgoing, "pw", split_axis=0, concat_axis=0, tiled=True)
        parts.append(jnp.einsum("dckz,zcbs->dbsk", forward, sticks_back, precision=fast))
    vpsi = jnp.concatenate(parts, axis=1)
    applied = kinetic[None, None] * psi_block + vpsi
    lowered = applied.astype(jnp.bfloat16)
    gathered = lax.all_gather(lowered, "band", axis=1, tiled=True)
    intersection = intersect(gathered, psi_all, pw_count)
    return (intersection, applied)


def per_device(psi_block, psi_all, potential, stick_col):
    return per_device_rows(psi_block, psi_all, potential, stick_col)


def solution(mesh):
    return jax.shard_map(
        per_device,
        mesh=mesh,
        in_specs=(
            P(None, "band", "pw", None),
            P(None, "band", "pw", None),
            P("pw", None, None),
            P(),
        ),
        out_specs=(P(None, "pw", "band"), P(None, "band", "pw", None)),
        check_vma=False,
    )
```

profile of v0, /device:TPU:0, one launch (start us, length us, event | category | flops | bytes accessed | tf_op | source)
XLA Modules:
  0.0 94.0 jit_solution(17449898297534052666)
XLA Ops:
  0.6 1.2 %convolution_bitcast_fusion.1 = f32[128,2,1,32]{0,3,1,2:T(8,128)S(1)} fusion(f32[2,2,128,128]{3,2,1,0:T(8,128)} %constant.89.clone, f32[2,2,32,128]{3,2,1,0:T(8,128)} %param.8), kind=kOutput, calls=%fused_computation.33 | convolution fusion | flops 12582912 | bytes 327680 | tf_op jit(solution)/shard_map/dczk,cbsk->zdbs/dot_general | solution.py:117
  2.7 7.3 %all-to-all-start.2 = ((f32[8,1,1024]{2,1,0:T(1,128)}), f32[8,1,1024]{2,1,0:T(1,128)S(1)}, u32[]{:S(2)}, u32[]{:S(2)}) async-start(f32[8,1,1024]{2,1,0:T(1,128)} %reshape.302), calls=%async_computation.2 | async-start | bytes 65536 | tf_op jit(solution)/shard_map/all_to_all | solution.py:118
  10.0 1.2 %convolution_bitcast_fusion.3 = f32[128,2,1,32]{0,3,1,2:T(8,128)S(1)} fusion(f32[2,2,128,128]{3,2,1,0:T(8,128)} %constant.89.clone, f32[2,2,32,128]{3,2,1,0:T(8,128)} %param.8), kind=kOutput, calls=%fused_computation.35 | convolution fusion | flops 12582912 | bytes 327680 | tf_op jit(solution)/shard_map/dczk,cbsk->zdbs/dot_general | solution.py:117
  13.4 4.1 %fusion.88 = (bf16[2,64,32,128]{3,2,1,0:T(8,128)(2,1)}, bf16[2,64,32,128]{3,2,1,0:T(8,128)(2,1)}, bf16[2,64,32,128]{3,2,1,0:T(8,128)(2,1)}, bf16[2,64,32,128]{3,2,1,0:T(8,128)(2,1)S(1)}) fusion(bf16[2,256,32,128]{3,2,1,0:T(8,128)(2,1)} %param.9), kind=kLoop, calls=%fused_computation.129 | loop fusion | bytes 8388608 | tf_op jit(solution)/shard_map/slice | solution.py:85
  17.6 6.0 %all-to-all-start = ((f32[8,1,1024]{2,1,0:T(1,128)}), f32[8,1,1024]{2,1,0:T(1,128)S(1)}, u32[]{:S(2)}, u32[]{:S(2)}) async-start(f32[8,1,1024]{2,1,0:T(1,128)} %reshape.300), calls=%async_computation | async-start | bytes 65536 | tf_op jit(solution)/shard_map/all_to_all | solution.py:118
  26.9 3.4 %all-to-all-done = f32[8,1,1024]{2,1,0:T(1,128)S(1)} async-done(((f32[8,1,1024]{2,1,0:T(1,128)}), f32[8,1,1024]{2,1,0:T(1,128)S(1)}, u32[]{:S(2)}, u32[]{:S(2)}) %all-to-all-start) | async-done | bytes 32800 | tf_op jit(solution)/shard_map/all_to_all | solution.py:118
  31.5 1.7 %fusion.12 = f32[16,128,128]{2,1,0:T(8,128)S(1)} fusion(f32[128,256]{1,0:T(8,128)} %copy-done.9, f32[16,256]{1,0:T(8,128)S(1)} %mul.266, f32[128,256]{1,0:T(8,128)S(1)} %get-tuple-element.30, f32[16,256]{1,0:T(8,128)S(1)} %mul.257, s32[256]{0:T(256)S(1)} %get-tuple-element.28), kind=kOutput, calls=%fused_computation.16 | convolution fusion | flops 404258816 | bytes 1344512 | tf_op jit(solution)/shard_map/dot_general | solution.py:47
  33.2 1.7 %fusion.8 = f32[16,128,128]{2,1,0:T(8,128)S(1)} fusion(f32[128,256]{1,0:T(8,128)} %copy-done.9, f32[16,256]{1,0:T(8,128)S(1)} %mul.266, f32[128,256]{1,0:T(8,128)S(1)} %get-tuple-element.30, f32[16,256]{1,0:T(8,128)S(1)} %mul.257, s32[256]{0:T(256)S(1)} %get-tuple-element.28), kind=kOutput, calls=%fused_computation.12 | convolution fusion | flops 404258816 | bytes 1344512 | tf_op jit(solution)/shard_map/dot_general | solution.py:47
  44.4 0.9 fusion.66
  45.3 1.7 %add_reduce_fusion.1 = (f32[16,256]{1,0:T(8,128)S(1)}, f32[16,256]{1,0:T(8,128)S(1)}, f32[16,256]{1,0:T(8,128)S(1)}, f32[16,256]{1,0:T(8,128)S(1)}) fusion(f32[16,128,256]{2,1,0:T(8,128)S(1)} %fusion.66, f32[128,256]{1,0:T(8,128)S(1)} %copy-done.10, f32[128,256]{1,0:T(8,128)S(1)} %get-tuple-element.30, f32[16,128,256]{2,1,0:T(8,128)S(1)} %fusion.62, ...), kind=kOutput, calls=%fused_computation.11 | convolution fusion | flops 411058176 | bytes 7668736 | tf_op jit(solution)/shard_map/dot_general | solution.py:47
  48.1 3.3 %all-to-all-start.1 = ((f32[8,1,1024]{2,1,0:T(1,128)}), f32[8,1,1024]{2,1,0:T(1,128)S(1)}, u32[]{:S(2)}, u32[]{:S(2)}) async-start(f32[8,1,1024]{2,1,0:T(1,128)} %reshape.306), calls=%async_computation.1 | async-start | bytes 65536 | tf_op jit(solution)/shard_map/all_to_all | solution.py:127
  52.5 5.5 %all-to-all-done.1 = f32[8,1,1024]{2,1,0:T(1,128)S(1)} async-done(((f32[8,1,1024]{2,1,0:T(1,128)}), f32[8,1,1024]{2,1,0:T(1,128)S(1)}, u32[]{:S(2)}, u32[]{:S(2)}) %all-to-all-start.1) | async-done | bytes 32800 | tf_op jit(solution)/shard_map/all_to_all | solution.py:127
  58.1 4.0 %all-to-all-start.3 = ((f32[8,1,1024]{2,1,0:T(1,128)}), f32[8,1,1024]{2,1,0:T(1,128)}, u32[]{:S(2)}, u32[]{:S(2)}) async-start(f32[8,1,1024]{2,1,0:T(1,128)} %reshape.304), calls=%async_computation.3 | async-start | bytes 65536 | tf_op jit(solution)/shard_map/all_to_all | solution.py:127
  62.1 1.4 %reduce.12 = f32[8,1024]{1,0:T(8,128)} reduce(f32[8,1,1024]{2,1,0:T(1,128)S(1)} %all-to-all-done.1, f32[]{:T(128)} %broadcast.248), dimensions={1}, to_apply=%all_to_all.16.reduce_sub_computation | reduce | bytes 65540 | tf_op jit(solution)/shard_map/all_to_all | solution.py:127
  63.5 0.9 reshape.307
  65.1 3.6 %all-to-all-done.3 = f32[8,1,1024]{2,1,0:T(1,128)} async-done(((f32[8,1,1024]{2,1,0:T(1,128)}), f32[8,1,1024]{2,1,0:T(1,128)}, u32[]{:S(2)}, u32[]{:S(2)}) %all-to-all-start.3) | async-done | bytes 32800 | tf_op jit(solution)/shard_map/all_to_all | solution.py:127
  68.7 2.1 %reduce.11 = f32[8,1024]{1,0:T(8,128)} reduce(f32[8,1,1024]{2,1,0:T(1,128)} %all-to-all-done.3, f32[]{:T(128)} %broadcast.248), dimensions={1}, to_apply=%all_to_all.18.reduce_sub_computation | reduce | bytes 65540 | tf_op jit(solution)/shard_map/all_to_all | solution.py:127
  70.8 0.9 reshape.305
  72.5 1.0 %convolution_bitcast_fusion.2 = f32[2,1,32,128]{3,2,0,1:T(8,128)S(1)} fusion(f32[2,2,128,128]{3,2,1,0:T(8,128)S(1)} %copy-done.3, f32[128,2,1,32]{0,3,1,2:T(8,128)} %copy.74), kind=kOutput, calls=%fused_computation.34 | convolution fusion | flops 12582912 | bytes 327680 | tf_op jit(solution)/shard_map/dckz,zcbs->dbsk/dot_general | solution.py:128
  73.5 1.0 %convolution_bitcast_fusion = f32[2,1,32,128]{3,2,0,1:T(8,128)S(1)} fusion(f32[2,2,128,128]{3,2,1,0:T(8,128)S(1)} %copy-done.3, f32[128,2,1,32]{0,3,1,2:T(8,128)} %copy.82), kind=kOutput, calls=%fused_computation.32 | convolution fusion | flops 12582912 | bytes 327680 | tf_op jit(solution)/shard_map/dckz,zcbs->dbsk/dot_general | solution.py:128
  74.5 0.9 fusion.87
  75.4 5.4 %all_gather.3 = bf16[2,8,32,128]{3,2,0,1:T(8,128)(2,1)S(1)} all-gather(bf16[2,2,32,128]{3,2,0,1:T(8,128)(2,1)S(1)} %get-tuple-element.16), channel_id=1, replica_groups=mesh['pw'=8,'band'=4] {'band'}, dimensions={1}, use_global_device_ids=true | all-gather | bytes 163840 | tf_op jit(solution)/shard_map/all_gather | solution.py:132
  83.6 3.3 %all-to-all-start.4 = ((f32[2,8,1,256]{3,0,2,1:T(2,128)}), f32[2,8,1,256]{3,0,2,1:T(2,128)S(1)}, u32[]{:S(2)}, u32[]{:S(2)}) async-start(f32[2,8,1,256]{3,0,2,1:T(2,128)} %copy.90), calls=%async_computation.4 | async-start | bytes 32768 | tf_op jit(solution)/shard_map/all_to_all | solution.py:98
  87.5 5.9 %all-to-all-done.4 = f32[2,8,1,256]{3,0,2,1:T(2,128)S(1)} async-done(((f32[2,8,1,256]{3,0,2,1:T(2,128)}), f32[2,8,1,256]{3,0,2,1:T(2,128)S(1)}, u32[]{:S(2)}, u32[]{:S(2)}) %all-to-all-start.4) | async-done | bytes 16416 | tf_op jit(solution)/shard_map/all_to_all | solution.py:98
  (92 shorter events, 24.4 us)
Async XLA Ops:
  2.7 14.9 %all-to-all-start.2 = ((f32[8,1,1024]{2,1,0:T(1,128)}), f32[8,1,1024]{2,1,0:T(1,128)S(1)}, u32[]{:S(2)}, u32[]{:S(2)}) async-start(f32[8,1,1024]{2,1,0:T(1,128)} %reshape.302), calls=%async_computation.2 | async-start | bytes 65536 | tf_op jit(solution)/shard_map/all_to_all | solution.py:118
  12.5 13.6 %copy-start.9 = (f32[128,256]{1,0:T(8,128)}, f32[128,256]{1,0:T(8,128)S(1)}, u32[]{:S(2)}) copy-start(f32[128,256]{1,0:T(8,128)S(1)} %get-tuple-element.31) | copy-start | bytes 393220
  13.4 4.1 %copy-start.11 = (s32[256]{0:T(256)S(1)}, s32[256]{0:T(256)}, u32[]{:S(2)}) copy-start(s32[256]{0:T(256)} %param.11) | copy-start | bytes 3076
  17.6 12.7 %all-to-all-start = ((f32[8,1,1024]{2,1,0:T(1,128)}), f32[8,1,1024]{2,1,0:T(1,128)S(1)}, u32[]{:S(2)}, u32[]{:S(2)}) async-start(f32[8,1,1024]{2,1,0:T(1,128)} %reshape.300), calls=%async_computation | async-start | bytes 65536 | tf_op jit(solution)/shard_map/all_to_all | solution.py:118
  31.3 3.5 %copy-start.2 = (f32[128,128,1]{1,0,2:T(8,128)S(1)}, f32[128,128,1]{1,0,2:T(8,128)}, u32[]{:S(2)}) copy-start(f32[128,128,1]{1,0,2:T(8,128)} %constant.101) | copy-start | bytes 196612
  34.9 1.2 %copy-start = (f32[16,128,128]{2,1,0:T(8,128)S(1)}, f32[16,128,128]{2,1,0:T(8,128)}, u32[]{:S(2)}) copy-start(f32[16,128,128]{2,1,0:T(8,128)} %param.10) | copy-start | bytes 3145732
  34.9 1.2 %copy-start.7 = (f32[128,128,1]{1,0,2:T(8,128)S(1)}, f32[128,128,1]{1,0,2:T(8,128)}, u32[]{:S(2)}) copy-start(f32[128,128,1]{1,0,2:T(8,128)} %constant.103) | copy-start | bytes 196612
  36.1 0.8 copy-start.1
  39.8 0.8 copy-start.8
  44.4 0.9 copy-start.10
  47.0 25.4 %copy-start.3 = (f32[2,2,128,128]{3,2,1,0:T(8,128)S(1)}, f32[2,2,128,128]{3,2,1,0:T(8,128)}, u32[]{:S(2)}) copy-start(f32[2,2,128,128]{3,2,1,0:T(8,128)} %constant.90.clone) | copy-start | bytes 786436
  47.2 33.7 %copy-start.6 = (bf16[2,64,32,128]{3,2,1,0:T(8,128)(2,1)S(1)}, bf16[2,64,32,128]{3,2,1,0:T(8,128)(2,1)}, u32[]{:S(2)}) copy-start(bf16[2,64,32,128]{3,2,1,0:T(8,128)(2,1)} %get-tuple-element.18) | copy-start | bytes 3145732
  48.1 10.0 %all-to-all-start.1 = ((f32[8,1,1024]{2,1,0:T(1,128)}), f32[8,1,1024]{2,1,0:T(1,128)S(1)}, u32[]{:S(2)}, u32[]{:S(2)}) async-start(f32[8,1,1024]{2,1,0:T(1,128)} %reshape.306), calls=%async_computation.1 | async-start | bytes 65536 | tf_op jit(solution)/shard_map/all_to_all | solution.py:127
  58.1 10.7 %all-to-all-start.3 = ((f32[8,1,1024]{2,1,0:T(1,128)}), f32[8,1,1024]{2,1,0:T(1,128)}, u32[]{:S(2)}, u32[]{:S(2)}) async-start(f32[8,1,1024]{2,1,0:T(1,128)} %reshape.304), calls=%async_computation.3 | async-start | bytes 65536 | tf_op jit(solution)/shard_map/all_to_all | solution.py:127
  62.1 19.2 %copy-start.5 = (bf16[2,64,32,128]{3,2,1,0:T(8,128)(2,1)S(1)}, bf16[2,64,32,128]{3,2,1,0:T(8,128)(2,1)}, u32[]{:S(2)}) copy-start(bf16[2,64,32,128]{3,2,1,0:T(8,128)(2,1)} %get-tuple-element.20) | copy-start | bytes 3145732
  80.8 1.2 %copy-start.4 = (bf16[2,64,32,128]{3,2,1,0:T(8,128)(2,1)S(1)}, bf16[2,64,32,128]{3,2,1,0:T(8,128)(2,1)}, u32[]{:S(2)}) copy-start(bf16[2,64,32,128]{3,2,1,0:T(8,128)(2,1)} %get-tuple-element.19) | copy-start | bytes 3145732
  83.6 9.8 %all-to-all-start.4 = ((f32[2,8,1,256]{3,0,2,1:T(2,128)}), f32[2,8,1,256]{3,0,2,1:T(2,128)S(1)}, u32[]{:S(2)}, u32[]{:S(2)}) async-start(f32[2,8,1,256]{3,0,2,1:T(2,128)} %copy.90), calls=%async_computation.4 | async-start | bytes 32768 | tf_op jit(solution)/shard_map/all_to_all | solution.py:98
where the time goes:
time: 95.2 us; the launch traced here: 94 us
  starting transfers between devices  23.9 us (25%)
  matrix products  22 us (23%)
  waiting for transfers between devices  18.4 us (19%)
  local copies, waits for them, and re-layouts  15.8 us (17%)
  other arithmetic  7.35 us (8%)
  blocking collectives  5.43 us (6%)
  between operations  1.15 us (1%)
    dot_general x20, matrix products, mult(): jnp.dot(left, right, precision=lax.Precision.HIGH, preferred_element_type...  15.8 us
    all_to_all x2, starting transfers between devices, per_device_rows(): lax.all_to_all(z_lines, 'pw', split_axis=0, concat_axis=0, tiled=True)  13.3 us
    all_to_all x2, waiting for transfers between devices, per_device_rows(): lax.all_to_all(outgoing, 'pw', split_axis=0, concat_axis=0, tiled=True)  9.14 us
    all_to_all x2, starting transfers between devices, per_device_rows(): lax.all_to_all(outgoing, 'pw', split_axis=0, concat_axis=0, tiled=True)  7.3 us
    unnamed x33, local copies, waits for them, and re-layouts  7.24 us
    all_to_all x1, waiting for transfers between devices, intersect(): lax.all_to_all(pieces, 'pw', split_axis=1, concat_axis=1, tiled=True)  5.88 us
    all_gather x1, blocking collectives, per_device_rows(): gathered = lax.all_gather(lowered, 'band', axis=1, tiled=True)  5.43 us
    slice x1, local copies, waits for them, and re-layouts, intersect(): psi_all[:, k * width:(k + 1) * width]  4.12 us
  transfers between devices with their start and end apart: 5, of which 4 were waited for; matrix products, arithmetic and copies ran while one was open for 17% of the time, Pallas kernels for 0%

commit v1 on v0

--- a/solution.py
+++ b/solution.py
@@ -4,6 +4,17 @@
 import jax.numpy as jnp
 from jax import lax
 from jax.sharding import PartitionSpec as P
+
+
+def in_blocks(array, dim, length):
+    before, after = (array.shape[:dim], array.shape[dim + 1 :])
+    return jnp.moveaxis(array.reshape(*before, length, -1, *after), dim, 0)
+
+
+def joined_along(blocks, dim):
+    blocks = jnp.moveaxis(blocks, 0, dim)
+    shape = blocks.shape
+    return blocks.reshape(*shape[:dim], shape[dim] * shape[dim + 1], *shape[dim + 2 :])
 
 
 def frequency(index, size):
@@ -115,7 +126,14 @@
     for band in range(psi_block.shape[1]):
         coeffs = psi_block[:, band : band + 1]
         z_lines = jnp.einsum("dczk,cbsk->zdbs", inverse, coeffs, precision=fast)
-        received = lax.all_to_all(z_lines, "pw", split_axis=0, concat_axis=0, tiled=True)
+        size_2, index_2 = (lax.axis_size("pw"), lax.axis_index("pw"))
+        blocks = in_blocks(z_lines, 0, size_2)
+        gathered_2 = [blocks[index_2]]
+        for step in range(1, size_2):
+            sent = blocks[index_2 ^ step]
+            gathered_2.append(lax.ppermute(sent, "pw", [(i, i ^ step) for i in range(size_2)]))
+        blocks = jnp.stack(gathered_2)[index_2 ^ jnp.arange(size_2)]
+        received = joined_along(blocks, 0)
         lanes = received.shape[1:]
         received = received.reshape((pw_count, planes) + lanes)
         amp = jnp.transpose(received, (2, 3, 1, 0, 4)).reshape(

time: 95.2 us -> 110 us (1.16)
  starting transfers between devices: 23.9 us -> 33.8 us
  local copies, waits for them, and re-layouts: 15.8 us -> 20.2 us
    ppermute x0 -> x14, starting transfers between devices: none -> 23.2 us  [per_device_rows(): lax.ppermute(sent, 'pw', [(i, i ^ step) for i in range(size_2)])]
    all_to_all x2 -> x0, starting transfers between devices: 13.3 us -> none  [per_device_rows(): lax.all_to_all(z_lines, 'pw', split_axis=0, concat_axis=0, tiled=True)]
    ppermute x0 -> x14, waiting for transfers between devices: none -> 4.28 us  [per_device_rows(): lax.ppermute(sent, 'pw', [(i, i ^ step) for i in range(size_2)])]
    all_to_all x2 -> x0, waiting for transfers between devices: 3.41 us -> none  [per_device_rows(): lax.all_to_all(z_lines, 'pw', split_axis=0, concat_axis=0, tiled=True)]
    unnamed x33 -> x51, local copies, waits for them, and re-layouts: 7.24 us -> 9.81 us
    all_to_all x2 -> x0, other arithmetic: 1.44 us -> none  [per_device_rows(): lax.all_to_all(z_lines, 'pw', split_axis=0, concat_axis=0, tiled=True)]
    gather x0 -> x2, local copies, waits for them, and re-layouts: none -> 1.11 us  [per_device_rows(): blocks = jnp.stack(gathered_2)[index_2 ^ jnp.arange(size_2)]]
  transfers between devices with their start and end apart: 5 -> 17, of which waited for: 4 -> 5; matrix products, arithmetic and copies ran while one was open for 17% -> 19% of each run, Pallas kernels for 0% -> 0%
where the time goes in v1:
time: 110 us; the launch traced here: 109 us
  starting transfers between devices  33.8 us (31%)
  matrix products  22.7 us (21%)
  local copies, waits for them, and re-layouts  20.2 us (18%)
  waiting for transfers between devices  18.9 us (17%)
  other arithmetic  6.91 us (6%)
  blocking collectives  5.43 us (5%)
  between operations  1.29 us (1%)
    ppermute x14, starting transfers between devices, per_device_rows(): lax.ppermute(sent, 'pw', [(i, i ^ step) for i in range(size_2)])  23.2 us
    dot_general x20, matrix products, mult(): jnp.dot(left, right, precision=lax.Precision.HIGH, preferred_element_type...  16.5 us
    unnamed x51, local copies, waits for them, and re-layouts  9.81 us
    all_to_all x2, waiting for transfers between devices, per_device_rows(): lax.all_to_all(outgoing, 'pw', split_axis=0, concat_axis=0, tiled=True)  8.7 us
    all_to_all x2, starting transfers between devices, per_device_rows(): lax.all_to_all(outgoing, 'pw', split_axis=0, concat_axis=0, tiled=True)  7.28 us
    all_to_all x1, waiting for transfers between devices, intersect(): lax.all_to_all(pieces, 'pw', split_axis=1, concat_axis=1, tiled=True)  5.88 us
    all_gather x1, blocking collectives, per_device_rows(): gathered = lax.all_gather(lowered, 'band', axis=1, tiled=True)  5.43 us
    ppermute x14, waiting for transfers between devices, per_device_rows(): lax.ppermute(sent, 'pw', [(i, i ^ step) for i in range(size_2)])  4.28 us
  transfers between devices with their start and end apart: 17, of which 5 were waited for; matrix products, arithmetic and copies ran while one was open for 19% of the time, Pallas kernels for 0%

profile of v1, /device:TPU:0, one launch (start us, length us, event | category | flops | bytes accessed | tf_op | source)
XLA Modules:
  0.0 109.1 jit_solution(5192806930592682557)
XLA Ops:
  2.1 3.0 %collective-permute-start.7 = (f32[16,2,1,32]{3,0,1,2:T(8,128)S(1)}, f32[16,2,1,32]{3,0,1,2:T(8,128)S(1)}, u32[]{:S(2)}, u32[]{:S(2)}) collective-permute-start(f32[16,2,1,32]{3,0,1,2:T(8,128)S(1)} %get-tuple-element.32), channel_id=1, source_target_pairs={{0,4},{4,0},{8,12},{12,8},{16,20},{20,16},{24,28},{28,24},{1,5},{5... | collective-permute-start | bytes 12296 | tf_op jit(solution)/shard_map/ppermute | solution.py:134
  5.1 1.6 %collective-permute-start.8 = (f32[16,2,1,32]{3,0,1,2:T(8,128)S(1)}, f32[16,2,1,32]{3,0,1,2:T(8,128)S(1)}, u32[]{:S(2)}, u32[]{:S(2)}) collective-permute-start(f32[16,2,1,32]{3,0,1,2:T(8,128)S(1)} %get-tuple-element.31), channel_id=1, source_target_pairs={{0,8},{4,12},{8,0},{12,4},{16,24},{20,28},{24,16},{28,20},{1,9},{5... | collective-permute-start | bytes 12296 | tf_op jit(solution)/shard_map/ppermute | solution.py:134
  6.7 3.0 %collective-permute-start.10 = (f32[16,2,1,32]{3,0,1,2:T(8,128)S(1)}, f32[16,2,1,32]{3,0,1,2:T(8,128)S(1)}, u32[]{:S(2)}, u32[]{:S(2)}) collective-permute-start(f32[16,2,1,32]{3,0,1,2:T(8,128)S(1)} %get-tuple-element.29), channel_id=1, source_target_pairs={{0,16},{4,20},{8,24},{12,28},{16,0},{20,4},{24,8},{28,12},{1,17},{... | collective-permute-start | bytes 12296 | tf_op jit(solution)/shard_map/ppermute | solution.py:134
  9.6 1.3 %collective-permute-start.11 = (f32[16,2,1,32]{3,0,1,2:T(8,128)S(1)}, f32[16,2,1,32]{3,0,1,2:T(8,128)S(1)}, u32[]{:S(2)}, u32[]{:S(2)}) collective-permute-start(f32[16,2,1,32]{3,0,1,2:T(8,128)S(1)} %get-tuple-element.28), channel_id=1, source_target_pairs={{0,20},{4,16},{8,28},{12,24},{16,4},{20,0},{24,12},{28,8},{1,21},{... | collective-permute-start | bytes 12296 | tf_op jit(solution)/shard_map/ppermute | solution.py:134
  14.7 4.2 %fusion.89 = (bf16[2,64,32,128]{3,2,1,0:T(8,128)(2,1)}, bf16[2,64,32,128]{3,2,1,0:T(8,128)(2,1)}, bf16[2,64,32,128]{3,2,1,0:T(8,128)(2,1)}, bf16[2,64,32,128]{3,2,1,0:T(8,128)(2,1)S(1)}) fusion(bf16[2,256,32,128]{3,2,1,0:T(8,128)(2,1)} %param.9), kind=kLoop, calls=%fused_computation.164 | loop fusion | bytes 8388608 | tf_op jit(solution)/shard_map/slice | solution.py:96
  19.5 3.6 %collective-permute-start.12 = (f32[16,2,1,32]{3,0,1,2:T(8,128)S(1)}, f32[16,2,1,32]{3,0,1,2:T(8,128)S(1)}, u32[]{:S(2)}, u32[]{:S(2)}) collective-permute-start(f32[16,2,1,32]{3,0,1,2:T(8,128)S(1)} %get-tuple-element.27), channel_id=1, source_target_pairs={{0,24},{4,28},{8,16},{12,20},{16,8},{20,12},{24,0},{28,4},{1,25},{... | collective-permute-start | bytes 12296 | tf_op jit(solution)/shard_map/ppermute | solution.py:134
  23.2 1.7 %collective-permute-start = (f32[16,2,1,32]{3,0,1,2:T(8,128)}, f32[16,2,1,32]{3,0,1,2:T(8,128)}, u32[]{:S(2)}, u32[]{:S(2)}) collective-permute-start(f32[16,2,1,32]{3,0,1,2:T(8,128)} %get-tuple-element.41), channel_id=1, source_target_pairs={{0,4},{4,0},{8,12},{12,8},{16,20},{20,16},{24,28},{28,24},{1,5},{5... | collective-permute-start | bytes 12296 | tf_op jit(solution)/shard_map/ppermute | solution.py:134
  24.9 1.9 %collective-permute-start.2 = (f32[16,2,1,32]{3,0,1,2:T(8,128)}, f32[16,2,1,32]{3,0,1,2:T(8,128)}, u32[]{:S(2)}, u32[]{:S(2)}) collective-permute-start(f32[16,2,1,32]{3,0,1,2:T(8,128)} %get-tuple-element.39), channel_id=1, source_target_pairs={{0,12},{4,8},{8,4},{12,0},{16,28},{20,24},{24,20},{28,16},{1,13},{... | collective-permute-start | bytes 12296 | tf_op jit(solution)/shard_map/ppermute | solution.py:134
  26.7 2.4 %collective-permute-start.3 = (f32[16,2,1,32]{3,0,1,2:T(8,128)}, f32[16,2,1,32]{3,0,1,2:T(8,128)}, u32[]{:S(2)}, u32[]{:S(2)}) collective-permute-start(f32[16,2,1,32]{3,0,1,2:T(8,128)} %get-tuple-element.38), channel_id=1, source_target_pairs={{0,16},{4,20},{8,24},{12,28},{16,0},{20,4},{24,8},{28,12},{1,17},{... | collective-permute-start | bytes 12296 | tf_op jit(solution)/shard_map/ppermute | solution.py:134
  32.9 1.5 %fusion.4 = f32[16,128,128]{2,1,0:T(8,128)S(1)} fusion(f32[16,256]{1,0:T(8,128)} %copy-done.12, f32[16,256]{1,0:T(8,128)} %copy-done.11, f32[128,256]{1,0:T(8,128)S(1)} %get-tuple-element.45, f32[128,256]{1,0:T(8,128)S(1)} %get-tuple-element.44, s32[256]{0:T(256)S(1)} %get-tuple-element.42), kind=kOutput, calls=%fused_computation.8 | convolution fusion | flops 404258816 | bytes 1344512 | tf_op jit(solution)/shard_map/dot_general | solution.py:58
  34.5 3.7 %collective-permute-start.5 = (f32[16,2,1,32]{3,0,1,2:T(8,128)}, f32[16,2,1,32]{3,0,1,2:T(8,128)S(1)}, u32[]{:S(2)}, u32[]{:S(2)}) collective-permute-start(f32[16,2,1,32]{3,0,1,2:T(8,128)} %get-tuple-element.36), channel_id=1, source_target_pairs={{0,24},{4,28},{8,16},{12,20},{16,8},{20,12},{24,0},{28,4},{1,25},{... | collective-permute-start | bytes 12296 | tf_op jit(solution)/shard_map/ppermute | solution.py:134
  41.9 3.7 %collective-permute-done.6 = f32[16,2,1,32]{3,0,1,2:T(8,128)S(1)} collective-permute-done((f32[16,2,1,32]{3,0,1,2:T(8,128)}, f32[16,2,1,32]{3,0,1,2:T(8,128)S(1)}, u32[]{:S(2)}, u32[]{:S(2)}) %collective-permute-start.6) | collective-permute-done | bytes 4128 | tf_op jit(solution)/shard_map/ppermute | solution.py:134
  46.4 1.7 %fusion.8 = f32[16,128,128]{2,1,0:T(8,128)S(1)} fusion(f32[128,256]{1,0:T(8,128)} %copy-done.9, f32[16,256]{1,0:T(8,128)S(1)} %mul.266, f32[128,256]{1,0:T(8,128)S(1)} %get-tuple-element.44, f32[16,256]{1,0:T(8,128)S(1)} %mul.257, s32[256]{0:T(256)S(1)} %get-tuple-element.42), kind=kOutput, calls=%fused_computation.14 | convolution fusion | flops 404258816 | bytes 1344512 | tf_op jit(solution)/shard_map/dot_general | solution.py:58
  48.1 1.7 %fusion.12 = f32[16,128,128]{2,1,0:T(8,128)S(1)} fusion(f32[128,256]{1,0:T(8,128)} %copy-done.9, f32[16,256]{1,0:T(8,128)S(1)} %mul.266, f32[128,256]{1,0:T(8,128)S(1)} %get-tuple-element.44, f32[16,256]{1,0:T(8,128)S(1)} %mul.257, s32[256]{0:T(256)S(1)} %get-tuple-element.42), kind=kOutput, calls=%fused_computation.18 | convolution fusion | flops 404258816 | bytes 1344512 | tf_op jit(solution)/shard_map/dot_general | solution.py:58
  60.4 1.6 %add_reduce_fusion.1 = (f32[16,256]{1,0:T(8,128)S(1)}, f32[16,256]{1,0:T(8,128)S(1)}, f32[16,256]{1,0:T(8,128)S(1)}, f32[16,256]{1,0:T(8,128)S(1)}) fusion(f32[16,128,256]{2,1,0:T(8,128)S(1)} %fusion.66, f32[128,256]{1,0:T(8,128)S(1)} %copy-done.10, f32[128,256]{1,0:T(8,128)S(1)} %get-tuple-element.44, f32[16,128,256]{2,1,0:T(8,128)S(1)} %fusion.62, ...), kind=kOutput, calls=%fused_computation.13 | convolution fusion | flops 411058176 | bytes 7668736 | tf_op jit(solution)/shard_map/dot_general | solution.py:58
  63.2 3.3 %all-to-all-start = ((f32[8,1,1024]{2,1,0:T(1,128)}), f32[8,1,1024]{2,1,0:T(1,128)S(1)}, u32[]{:S(2)}, u32[]{:S(2)}) async-start(f32[8,1,1024]{2,1,0:T(1,128)} %reshape.338), calls=%async_computation | async-start | bytes 65536 | tf_op jit(solution)/shard_map/all_to_all | solution.py:145
  67.6 5.5 %all-to-all-done = f32[8,1,1024]{2,1,0:T(1,128)S(1)} async-done(((f32[8,1,1024]{2,1,0:T(1,128)}), f32[8,1,1024]{2,1,0:T(1,128)S(1)}, u32[]{:S(2)}, u32[]{:S(2)}) %all-to-all-start) | async-done | bytes 32800 | tf_op jit(solution)/shard_map/all_to_all | solution.py:145
  73.2 4.0 %all-to-all-start.1 = ((f32[8,1,1024]{2,1,0:T(1,128)}), f32[8,1,1024]{2,1,0:T(1,128)}, u32[]{:S(2)}, u32[]{:S(2)}) async-start(f32[8,1,1024]{2,1,0:T(1,128)} %reshape.336), calls=%async_computation.1 | async-start | bytes 65536 | tf_op jit(solution)/shard_map/all_to_all | solution.py:145
  77.7 1.3 %reduce.10 = f32[8,1024]{1,0:T(8,128)} reduce(f32[8,1,1024]{2,1,0:T(1,128)S(1)} %all-to-all-done, f32[]{:T(128)} %broadcast.293), dimensions={1}, to_apply=%all_to_all.9.reduce_sub_computation | reduce | bytes 65540 | tf_op jit(solution)/shard_map/all_to_all | solution.py:145
  80.6 3.2 %all-to-all-done.1 = f32[8,1,1024]{2,1,0:T(1,128)} async-done(((f32[8,1,1024]{2,1,0:T(1,128)}), f32[8,1,1024]{2,1,0:T(1,128)}, u32[]{:S(2)}, u32[]{:S(2)}) %all-to-all-start.1) | async-done | bytes 32800 | tf_op jit(solution)/shard_map/all_to_all | solution.py:145
  83.8 2.1 %reduce.9 = f32[8,1024]{1,0:T(8,128)} reduce(f32[8,1,1024]{2,1,0:T(1,128)} %all-to-all-done.1, f32[]{:T(128)} %broadcast.293), dimensions={1}, to_apply=%all_to_all.10.reduce_sub_computation | reduce | bytes 65540 | tf_op jit(solution)/shard_map/all_to_all | solution.py:145
  90.5 5.4 %all_gather.3 = bf16[2,8,32,128]{3,2,0,1:T(8,128)(2,1)S(1)} all-gather(bf16[2,2,32,128]{3,2,0,1:T(8,128)(2,1)S(1)} %get-tuple-element.16), channel_id=1, replica_groups=mesh['pw'=8,'band'=4] {'band'}, dimensions={1}, use_global_device_ids=true | all-gather | bytes 163840 | tf_op jit(solution)/shard_map/all_gather | solution.py:150
  98.7 3.3 %all-to-all-start.2 = ((f32[2,8,1,256]{3,0,2,1:T(2,128)}), f32[2,8,1,256]{3,0,2,1:T(2,128)S(1)}, u32[]{:S(2)}, u32[]{:S(2)}) async-start(f32[2,8,1,256]{3,0,2,1:T(2,128)} %copy.94), calls=%async_computation.2 | async-start | bytes 32768 | tf_op jit(solution)/shard_map/all_to_all | solution.py:109
  102.6 5.9 %all-to-all-done.2 = f32[2,8,1,256]{3,0,2,1:T(2,128)S(1)} async-done(((f32[2,8,1,256]{3,0,2,1:T(2,128)}), f32[2,8,1,256]{3,0,2,1:T(2,128)S(1)}, u32[]{:S(2)}, u32[]{:S(2)}) %all-to-all-start.2) | async-done | bytes 16416 | tf_op jit(solution)/shard_map/all_to_all | solution.py:109
  (138 shorter events, 37.4 us)
Async XLA Ops:
  2.1 17.5 %collective-permute-start.7 = (f32[16,2,1,32]{3,0,1,2:T(8,128)S(1)}, f32[16,2,1,32]{3,0,1,2:T(8,128)S(1)}, u32[]{:S(2)}, u32[]{:S(2)}) collective-permute-start(f32[16,2,1,32]{3,0,1,2:T(8,128)S(1)} %get-tuple-element.32), channel_id=1, source_target_pairs={{0,4},{4,0},{8,12},{12,8},{16,20},{20,16},{24,28},{28,24},{1,5},{5... | collective-permute-start | bytes 12296 | tf_op jit(solution)/shard_map/ppermute | solution.py:134
  5.1 18.1 %collective-permute-start.8 = (f32[16,2,1,32]{3,0,1,2:T(8,128)S(1)}, f32[16,2,1,32]{3,0,1,2:T(8,128)S(1)}, u32[]{:S(2)}, u32[]{:S(2)}) collective-permute-start(f32[16,2,1,32]{3,0,1,2:T(8,128)S(1)} %get-tuple-element.31), channel_id=1, source_target_pairs={{0,8},{4,12},{8,0},{12,4},{16,24},{20,28},{24,16},{28,20},{1,9},{5... | collective-permute-start | bytes 12296 | tf_op jit(solution)/shard_map/ppermute | solution.py:134
  6.7 16.5 %collective-permute-start.9 = (f32[16,2,1,32]{3,0,1,2:T(8,128)S(1)}, f32[16,2,1,32]{3,0,1,2:T(8,128)S(1)}, u32[]{:S(2)}, u32[]{:S(2)}) collective-permute-start(f32[16,2,1,32]{3,0,1,2:T(8,128)S(1)} %get-tuple-element.30), channel_id=1, source_target_pairs={{0,12},{4,8},{8,4},{12,0},{16,28},{20,24},{24,20},{28,16},{1,13},{... | collective-permute-start | bytes 12296 | tf_op jit(solution)/shard_map/ppermute | solution.py:134
  6.7 18.2 %collective-permute-start.10 = (f32[16,2,1,32]{3,0,1,2:T(8,128)S(1)}, f32[16,2,1,32]{3,0,1,2:T(8,128)S(1)}, u32[]{:S(2)}, u32[]{:S(2)}) collective-permute-start(f32[16,2,1,32]{3,0,1,2:T(8,128)S(1)} %get-tuple-element.29), channel_id=1, source_target_pairs={{0,16},{4,20},{8,24},{12,28},{16,0},{20,4},{24,8},{28,12},{1,17},{... | collective-permute-start | bytes 12296 | tf_op jit(solution)/shard_map/ppermute | solution.py:134
  9.6 15.2 %collective-permute-start.11 = (f32[16,2,1,32]{3,0,1,2:T(8,128)S(1)}, f32[16,2,1,32]{3,0,1,2:T(8,128)S(1)}, u32[]{:S(2)}, u32[]{:S(2)}) collective-permute-start(f32[16,2,1,32]{3,0,1,2:T(8,128)S(1)} %get-tuple-element.28), channel_id=1, source_target_pairs={{0,20},{4,16},{8,28},{12,24},{16,4},{20,0},{24,12},{28,8},{1,21},{... | collective-permute-start | bytes 12296 | tf_op jit(solution)/shard_map/ppermute | solution.py:134
  14.7 18.3 %copy-start.9 = (f32[128,256]{1,0:T(8,128)}, f32[128,256]{1,0:T(8,128)S(1)}, u32[]{:S(2)}) copy-start(f32[128,256]{1,0:T(8,128)S(1)} %get-tuple-element.45) | copy-start | bytes 393220
  14.7 4.2 %copy-start.13 = (s32[256]{0:T(256)S(1)}, s32[256]{0:T(256)}, u32[]{:S(2)}) copy-start(s32[256]{0:T(256)} %param.11) | copy-start | bytes 3076
  19.5 7.2 %collective-permute-start.12 = (f32[16,2,1,32]{3,0,1,2:T(8,128)S(1)}, f32[16,2,1,32]{3,0,1,2:T(8,128)S(1)}, u32[]{:S(2)}, u32[]{:S(2)}) collective-permute-start(f32[16,2,1,32]{3,0,1,2:T(8,128)S(1)} %get-tuple-element.27), channel_id=1, source_target_pairs={{0,24},{4,28},{8,16},{12,20},{16,8},{20,12},{24,0},{28,4},{1,25},{... | collective-permute-start | bytes 12296 | tf_op jit(solution)/shard_map/ppermute | solution.py:134
  23.1 6.5 %collective-permute-start.13 = (f32[16,2,1,32]{3,0,1,2:T(8,128)S(1)}, f32[16,2,1,32]{3,0,1,2:T(8,128)S(1)}, u32[]{:S(2)}, u32[]{:S(2)}) collective-permute-start(f32[16,2,1,32]{3,0,1,2:T(8,128)S(1)} %get-tuple-element.26), channel_id=1, source_target_pairs={{0,28},{4,24},{8,20},{12,16},{16,12},{20,8},{24,4},{28,0},{1,29},{... | collective-permute-start | bytes 12296 | tf_op jit(solution)/shard_map/ppermute | solution.py:134
  23.2 11.3 %collective-permute-start = (f32[16,2,1,32]{3,0,1,2:T(8,128)}, f32[16,2,1,32]{3,0,1,2:T(8,128)}, u32[]{:S(2)}, u32[]{:S(2)}) collective-permute-start(f32[16,2,1,32]{3,0,1,2:T(8,128)} %get-tuple-element.41), channel_id=1, source_target_pairs={{0,4},{4,0},{8,12},{12,8},{16,20},{20,16},{24,28},{28,24},{1,5},{5... | collective-permute-start | bytes 12296 | tf_op jit(solution)/shard_map/ppermute | solution.py:134
  24.8 14.0 %collective-permute-start.1 = (f32[16,2,1,32]{3,0,1,2:T(8,128)}, f32[16,2,1,32]{3,0,1,2:T(8,128)}, u32[]{:S(2)}, u32[]{:S(2)}) collective-permute-start(f32[16,2,1,32]{3,0,1,2:T(8,128)} %get-tuple-element.40), channel_id=1, source_target_pairs={{0,8},{4,12},{8,0},{12,4},{16,24},{20,28},{24,16},{28,20},{1,9},{5... | collective-permute-start | bytes 12296 | tf_op jit(solution)/shard_map/ppermute | solution.py:134
  24.9 14.8 %collective-permute-start.2 = (f32[16,2,1,32]{3,0,1,2:T(8,128)}, f32[16,2,1,32]{3,0,1,2:T(8,128)}, u32[]{:S(2)}, u32[]{:S(2)}) collective-permute-start(f32[16,2,1,32]{3,0,1,2:T(8,128)} %get-tuple-element.39), channel_id=1, source_target_pairs={{0,12},{4,8},{8,4},{12,0},{16,28},{20,24},{24,20},{28,16},{1,13},{... | collective-permute-start | bytes 12296 | tf_op jit(solution)/shard_map/ppermute | solution.py:134
  26.7 13.7 %collective-permute-start.3 = (f32[16,2,1,32]{3,0,1,2:T(8,128)}, f32[16,2,1,32]{3,0,1,2:T(8,128)}, u32[]{:S(2)}, u32[]{:S(2)}) collective-permute-start(f32[16,2,1,32]{3,0,1,2:T(8,128)} %get-tuple-element.38), channel_id=1, source_target_pairs={{0,16},{4,20},{8,24},{12,28},{16,0},{20,4},{24,8},{28,12},{1,17},{... | collective-permute-start | bytes 12296 | tf_op jit(solution)/shard_map/ppermute | solution.py:134
  29.7 11.4 %collective-permute-start.4 = (f32[16,2,1,32]{3,0,1,2:T(8,128)}, f32[16,2,1,32]{3,0,1,2:T(8,128)}, u32[]{:S(2)}, u32[]{:S(2)}) collective-permute-start(f32[16,2,1,32]{3,0,1,2:T(8,128)} %get-tuple-element.37), channel_id=1, source_target_pairs={{0,20},{4,16},{8,28},{12,24},{16,4},{20,0},{24,12},{28,8},{1,21},{... | collective-permute-start | bytes 12296 | tf_op jit(solution)/shard_map/ppermute | solution.py:134
  34.5 7.4 %collective-permute-start.5 = (f32[16,2,1,32]{3,0,1,2:T(8,128)}, f32[16,2,1,32]{3,0,1,2:T(8,128)S(1)}, u32[]{:S(2)}, u32[]{:S(2)}) collective-permute-start(f32[16,2,1,32]{3,0,1,2:T(8,128)} %get-tuple-element.36), channel_id=1, source_target_pairs={{0,24},{4,28},{8,16},{12,20},{16,8},{20,12},{24,0},{28,4},{1,25},{... | collective-permute-start | bytes 12296 | tf_op jit(solution)/shard_map/ppermute | solution.py:134
  38.9 6.6 %collective-permute-start.6 = (f32[16,2,1,32]{3,0,1,2:T(8,128)}, f32[16,2,1,32]{3,0,1,2:T(8,128)S(1)}, u32[]{:S(2)}, u32[]{:S(2)}) collective-permute-start(f32[16,2,1,32]{3,0,1,2:T(8,128)} %get-tuple-element.35), channel_id=1, source_target_pairs={{0,28},{4,24},{8,20},{12,16},{16,12},{20,8},{24,4},{28,0},{1,29},{... | collective-permute-start | bytes 12296 | tf_op jit(solution)/shard_map/ppermute | solution.py:134
  62.1 15.0 %copy-start.14 = (f32[128]{0:T(128)S(1)}, f32[128]{0:T(128)}, u32[]{:S(2)}) copy-start(f32[128]{0:T(128)} %fusion.86) | copy-start | bytes 1540
  62.1 15.0 %copy-start.15 = (f32[32]{0:T(128)S(1)}, f32[32]{0:T(128)}, u32[]{:S(2)}) copy-start(f32[32]{0:T(128)} %fusion.82) | copy-start | bytes 388
  62.1 25.4 %copy-start.3 = (f32[2,2,128,128]{3,2,1,0:T(8,128)S(1)}, f32[2,2,128,128]{3,2,1,0:T(8,128)}, u32[]{:S(2)}) copy-start(f32[2,2,128,128]{3,2,1,0:T(8,128)} %constant.106.clone) | copy-start | bytes 786436
  62.3 33.7 %copy-start.6 = (bf16[2,64,32,128]{3,2,1,0:T(8,128)(2,1)S(1)}, bf16[2,64,32,128]{3,2,1,0:T(8,128)(2,1)}, u32[]{:S(2)}) copy-start(bf16[2,64,32,128]{3,2,1,0:T(8,128)(2,1)} %get-tuple-element.18) | copy-start | bytes 3145732
  63.2 10.0 %all-to-all-start = ((f32[8,1,1024]{2,1,0:T(1,128)}), f32[8,1,1024]{2,1,0:T(1,128)S(1)}, u32[]{:S(2)}, u32[]{:S(2)}) async-start(f32[8,1,1024]{2,1,0:T(1,128)} %reshape.338), calls=%async_computation | async-start | bytes 65536 | tf_op jit(solution)/shard_map/all_to_all | solution.py:145
  73.2 10.7 %all-to-all-start.1 = ((f32[8,1,1024]{2,1,0:T(1,128)}), f32[8,1,1024]{2,1,0:T(1,128)}, u32[]{:S(2)}, u32[]{:S(2)}) async-start(f32[8,1,1024]{2,1,0:T(1,128)} %reshape.336), calls=%async_computation.1 | async-start | bytes 65536 | tf_op jit(solution)/shard_map/all_to_all | solution.py:145
  77.2 19.2 %copy-start.5 = (bf16[2,64,32,128]{3,2,1,0:T(8,128)(2,1)S(1)}, bf16[2,64,32,128]{3,2,1,0:T(8,128)(2,1)}, u32[]{:S(2)}) copy-start(bf16[2,64,32,128]{3,2,1,0:T(8,128)(2,1)} %get-tuple-element.20) | copy-start | bytes 3145732
  98.7 9.9 %all-to-all-start.2 = ((f32[2,8,1,256]{3,0,2,1:T(2,128)}), f32[2,8,1,256]{3,0,2,1:T(2,128)S(1)}, u32[]{:S(2)}, u32[]{:S(2)}) async-start(f32[2,8,1,256]{3,0,2,1:T(2,128)} %copy.94), calls=%async_computation.2 | async-start | bytes 32768 | tf_op jit(solution)/shard_map/all_to_all | solution.py:109
  (9 other events, 11.0 us)
